TPU v7x, 512 devices: a whole 4x8x8 slice. The times are simulated.
512 devices in a mesh: group: 64 (over z, y), mp: 8 (over x, core).
Axes of the slice: x: 4, y: 8, z: 8, core: 2. Of those that a mesh axis runs over, the one named last changes fastest.
Arguments:
- tokens: bfloat16 [8192, 4096], P('group', 'mp'), may hold values from -3000 to 3000
- attn_gain: float32 [4096], replicated, may hold values from 0.1 to 1.9
- q_weight: bfloat16 [4096, 4096], P('group', 'mp'), may hold values from -0.09375 to 0.09375
- k_weight: bfloat16 [4096, 512], P('group'), may hold values from -0.09375 to 0.09375
- v_weight: bfloat16 [4096, 512], P('group'), may hold values from -0.09375 to 0.09375
- kv_pool: bfloat16 [4096, 8, 2, 16, 128], P('group', 'mp'), may hold values from -1000 to 1000
- page_table: int32 [256, 16], replicated, may hold values from 0 to 4095, as said below
- lengths: int32 [256], P('group'), may hold values from 2 to 256
- token_request: int32 [8192], P('group'), may hold values from 0 to 3
Outputs:
- attention: bfloat16 [8192, 4096], P('group', 'mp')
- decode_cache: bfloat16 [256, 8, 2, 256, 128], P('group', 'mp')
Inputs may be any that keep to these rules, and one draw needn't show every extreme that they name: Every pool page stands in exactly one slot of page_table. The pages that one group index holds for the requests of one owner (requests o * 4 to (o + 1) * 4 - 1) number at most 2, and exactly 2 for some pairs of holder and owner.
All inputs are finite; a program needn't handle non-finite values.
Results may differ from a plain program's by a relative error of at most 0.038.
Values may be sent and summed in bfloat16 or wider, within the bound.
No kernel may reach another device: no remote copies, remote signals or barrier semaphores. Data moves between devices by JAX's collectives and lax.ppermute only.
A program may use at most 64 MiB of HBM per device.

v0:
```python
import jax
import jax.numpy as jnp
from jax import lax
from jax.sharding import PartitionSpec as P

HEADS = 32
KVH = 4
rope_theta = 5000000.0
norm_eps = 1e-05


def from_partner(x, axis, bit):
    return lax.ppermute(x, axis, [(i, i ^ 1 << bit) for i in range(lax.axis_size(axis))])


def rotate(vectors, position):
    half_dim = vectors.shape[-1] // 2
    frequency = rope_theta ** (-(jnp.arange(half_dim, dtype=jnp.float32) / half_dim))
    angles = position.astype(jnp.float32)[:, None, None] * frequency[None, None, :]
    cosine = jnp.cos(angles)
    sine_part = jnp.sin(angles)
    first_half = vectors[..., :half_dim]
    second = vectors[..., half_dim:]
    return jnp.concatenate(
        [first_half * cosine - second * sine_part, second * cosine + first_half * sine_part],
        axis=-1,
    )


def normalize(group_rows, attn_gain):
    features = group_rows.astype(jnp.float32)
    root_mean = jnp.sqrt(jnp.mean(features * features, axis=-1, keepdims=True) + norm_eps)
    return (features / root_mean * attn_gain).astype(jnp.bfloat16)


def token_positions(token_request, group_lengths, request_count):
    member = (token_request[:, None] == jnp.arange(request_count, dtype=jnp.int32)[None, :]).astype(
        jnp.int32
    )
    earlier = jnp.sum((jnp.cumsum(member, axis=0) - member) * member, axis=1)
    return jnp.sum(member * group_lengths[None, :], axis=1) + earlier


def build_mask(token_request, group_lengths, max_len):
    request_count = group_lengths.shape[0]
    key_index = jnp.arange(request_count * max_len, dtype=jnp.int32)
    key_request = key_index // max_len
    key_alive = key_index % max_len < group_lengths[key_request]
    cached = (token_request[:, None] == key_request[None, :]) & key_alive[None, :]
    token_order = jnp.arange(token_request.shape[0], dtype=jnp.int32)
    fresh = (token_request[:, None] == token_request[None, :]) & (
        token_order[None, :] <= token_order[:, None]
    )
    return jnp.concatenate([cached, fresh], axis=1)


def weigh(scores, allowed):
    masked = jnp.where(allowed, scores, -1e30)
    row_top = jnp.max(masked, axis=-1, keepdims=True)
    exponent = jnp.exp(masked - row_top)
    return (exponent / jnp.sum(exponent, axis=-1, keepdims=True)).astype(jnp.bfloat16)


def on_device(
    tokens, attn_gain, q_weight, k_weight, v_weight, kv_pool, page_table, lengths, token_request
):
    groups = lax.axis_size("group")
    group_idx = lax.axis_index("group")
    mp_idx = lax.axis_index("mp")
    pool_pages = kv_pool.shape[0]
    pair_count = kv_pool.shape[1]
    page_len = kv_pool.shape[3]
    head_dim = kv_pool.shape[4]
    requests_here = lengths.shape[0]
    slot_count = pool_pages // requests_here
    max_len = slot_count * page_len
    capacity = 2 * pool_pages // groups
    flat_table = page_table.reshape(-1)
    slot_ids = jnp.arange(flat_table.shape[0], dtype=jnp.int32)
    owner_slot = jnp.zeros((flat_table.shape[0],), jnp.int32).at[flat_table].set(slot_ids)
    held_slots = lax.dynamic_slice_in_dim(owner_slot, group_idx * pool_pages, pool_pages)
    target_owner = held_slots // pool_pages
    slot_local = held_slots % pool_pages
    owner_hits = (target_owner[:, None] == jnp.arange(groups, dtype=jnp.int32)[None, :]).astype(
        jnp.int32
    )
    order_within = jnp.sum((jnp.cumsum(owner_hits, axis=0) - owner_hits) * owner_hits, axis=1)
    buffer_row = target_owner * capacity + order_within
    page_rows = kv_pool.reshape(pool_pages, -1)
    row_width = page_rows.shape[1]
    outgoing = (
        jnp.zeros((groups * capacity, row_width), jnp.bfloat16)
        .at[buffer_row]
        .set(page_rows)
        .reshape(groups, capacity, row_width)
    )
    outgoing_slots = (
        jnp.full((groups * capacity,), -1, jnp.int32)
        .at[buffer_row]
        .set(slot_local)
        .reshape(groups, capacity)
    )
    arrived, arrived_slots = (
        lax.all_to_all(outgoing, "group", split_axis=0, concat_axis=0, tiled=True),
        lax.all_to_all(outgoing_slots, "group", split_axis=0, concat_axis=0, tiled=True),
    )
    landing = jnp.where(arrived_slots < 0, pool_pages, arrived_slots).reshape(-1)
    placed = (
        jnp.zeros((pool_pages + 1, row_width), jnp.bfloat16)
        .at[landing]
        .set(arrived.reshape(-1, row_width))[:pool_pages]
    )
    decoded = placed.reshape(requests_here, slot_count, pair_count, 2, page_len, head_dim)
    decoded = decoded.transpose(0, 2, 3, 1, 4, 5).reshape(
        requests_here, pair_count, 2, max_len, head_dim
    )
    alive_mask = jnp.arange(max_len, dtype=jnp.int32)[None, :] < lengths[:, None]
    decoded = jnp.where(alive_mask[:, None, None, :, None], decoded, jnp.zeros((), jnp.bfloat16))
    whole_rows = lax.all_gather(tokens, "mp", axis=1, tiled=True)
    normed = normalize(whole_rows, attn_gain)
    rows_here = tokens.shape[0]
    heads_here = q_weight.shape[1] // head_dim
    per_kv = HEADS // KVH
    first_kv = mp_idx * heads_here // per_kv
    key_cols = lax.dynamic_slice_in_dim(k_weight, first_kv * head_dim, head_dim, 1)
    value_cols = lax.dynamic_slice_in_dim(v_weight, first_kv * head_dim, head_dim, 1)
    query_sum = jnp.dot(
        normed,
        lax.all_gather(q_weight, "group", axis=0, tiled=True),
        preferred_element_type=jnp.float32,
    )
    key_sum = jnp.dot(
        normed,
        lax.all_gather(key_cols, "group", axis=0, tiled=True),
        preferred_element_type=jnp.float32,
    )
    value_sum = jnp.dot(
        normed,
        lax.all_gather(value_cols, "group", axis=0, tiled=True),
        preferred_element_type=jnp.float32,
    )
    position = token_positions(token_request, lengths, requests_here)
    queries = (
        rotate(query_sum.reshape(rows_here, heads_here, head_dim), position)
        .astype(jnp.bfloat16)
        .transpose(1, 0, 2)
    )
    new_keys = rotate(key_sum.reshape(rows_here, 1, head_dim), position).astype(jnp.bfloat16)[:, 0]
    new_values = value_sum.astype(jnp.bfloat16)
    allowed = build_mask(token_request, lengths, max_len)
    score_scale = head_dim ** (-0.5)
    partner_cache = from_partner(decoded, "mp", 0)
    is_even = mp_idx % 2 == 0
    layer_zero = jnp.where(is_even, decoded, partner_cache)[:, 0]
    all_keys = jnp.concatenate(
        [layer_zero[:, 0].reshape(requests_here * max_len, head_dim), new_keys], axis=0
    )
    all_values = jnp.concatenate(
        [layer_zero[:, 1].reshape(requests_here * max_len, head_dim), new_values], axis=0
    )

    def attend(query_one):
        scores = (
            jnp.einsum("td,nd->tn", query_one, all_keys, preferred_element_type=jnp.float32)
            * score_scale
        )
        attn_probs = weigh(scores, allowed)
        return jnp.dot(attn_probs, all_values, preferred_element_type=jnp.float32).astype(
            jnp.bfloat16
        )

    heads_out = lax.map(attend, queries)
    attention = heads_out.transpose(1, 0, 2).reshape(rows_here, heads_here * head_dim)
    return (attention, partner_cache)


def solution(mesh):
    return jax.shard_map(
        on_device,
        mesh=mesh,
        in_specs=(
            P("group", "mp"),
            P(),
            P("group", "mp"),
            P("group", None),
            P("group", None),
            P("group", "mp", None, None, None),
            P(),
            P("group"),
            P("group"),
        ),
        out_specs=(P("group", "mp"), P("group", "mp", None, None, None)),
        check_vma=False,
    )
```

profile of v0, /device:TPU:2, one launch (start us, length us, event | category | flops | bytes accessed | tf_op | source)
XLA Modules:
  0.0 325.8 jit_solution(18150802313634479583)
XLA Ops:
  8.7 1.3 constant_dynamic-slice_fusion
  10.6 0.8 copy.29
  11.6 15.5 %scatter_custom_fusion = s32[4096]{0:T(1024)S(1)} fusion(s32[4096]{0:T(1024)S(1)} %bitcast.75, s32[4096]{0:T(1024)S(1)} %iota.46, s32[]{:T(128)} %copy.64), kind=kCustom, calls=%fused_computation.79 | custom fusion | bytes 16388 | tf_op jit(solution)/shard_map/scatter | solution.py:80
  29.2 16.6 %all-to-all-start = ((s32[64,1,2]{2,1,0:T(1,128)}), s32[64,1,2]{2,1,0:T(1,128)S(1)}, u32[]{:S(2)}, u32[]{:S(2)}) async-start(s32[64,1,2]{2,1,0:T(1,128)} %bitcast.4), calls=%async_computation | async-start | bytes 65536 | tf_op jit(solution)/shard_map/all_to_all | solution.py:105
  46.8 1.5 fusion.45
  48.2 2.6 compare_select_fusion.2
  50.8 0.9 select_reduce_fusion
  51.7 0.8 fusion.17
  53.5 2.3 scatter_custom_fusion.2
  55.8 1.5 reshape.342
  57.8 12.4 %all-to-all-start.1 = ((bf16[64,2,4096]{2,1,0:T(2,128)(2,1)}), bf16[64,2,4096]{2,1,0:T(2,128)(2,1)S(1)}, u32[]{:S(2)}, u32[]{:S(2)}) async-start(bf16[64,2,4096]{2,1,0:T(2,128)(2,1)} %reshape.342), calls=%async_computation.1 | async-start | bytes 2097152 | tf_op jit(solution)/shard_map/all_to_all | solution.py:104
  71.8 1.5 fusion.7
  73.4 1.6 fusion.9
  74.9 24.7 %all-to-all-done.1 = bf16[64,2,4096]{2,1,0:T(2,128)(2,1)S(1)} async-done(((bf16[64,2,4096]{2,1,0:T(2,128)(2,1)}), bf16[64,2,4096]{2,1,0:T(2,128)(2,1)S(1)}, u32[]{:S(2)}, u32[]{:S(2)}) %all-to-all-start.1) | async-done | bytes 1048608 | tf_op jit(solution)/shard_map/all_to_all | solution.py:104
  99.7 1.2 reshape.387
  100.9 2.8 scatter_custom_fusion.3
  104.1 2.1 collective-permute-start
  106.2 35.6 %all-gather.9.cloned.1.call-done = bf16[4096,128]{1,0:T(8,128)(2,1)} async-done(((bf16[64,128]{1,0:T(8,128)(2,1)}), bf16[4096,128]{1,0:T(8,128)(2,1)}) %all-gather.9.cloned.1.call-update) | async-done | bytes 1048592 | tf_op jit(solution)/shard_map/all_gather | solution.py:134
  141.8 1.7 convolution_bitcast_fusion
  143.9 80.1 %all-gather.11.cloned.1.call-done = bf16[4096,128]{1,0:T(8,128)(2,1)} async-done(((bf16[64,128]{1,0:T(8,128)(2,1)}), bf16[4096,128]{1,0:T(8,128)(2,1)}) %all-gather.11.cloned.1.call-update) | async-done | bytes 1048592 | tf_op jit(solution)/shard_map/all_gather | solution.py:139
  224.0 1.6 convolution_convert_fusion.1
  226.0 84.7 %all-gather.7.cloned.1.call-done = bf16[4096,512]{1,0:T(8,128)(2,1)} async-done(((bf16[64,512]{1,0:T(8,128)(2,1)}), bf16[4096,512]{1,0:T(8,128)(2,1)}) %all-gather.7.cloned.1.call-update) | async-done | bytes 4194320 | tf_op jit(solution)/shard_map/all_gather | solution.py:129
  310.6 2.9 fusion.46
  314.1 3.8 %while.10 = (s32[]{:T(128)}, bf16[4,128,128]{2,1,0:T(8,128)(2,1)S(1)}, bf16[4,128,128]{2,1,0:T(8,128)(2,1)S(1)}, bf16[1152,128]{1,0:T(8,128)(2,1)S(1)}, pred[128...) while((s32[]{:T(128)}, bf16[4,128,128]{2,1,0:T(8,128)(2,1)S(1)}, ...), condition=%wide.region_13.14_spmd, body=%wide.region_10.13_spmd.sunk | while | flops 76693248 | bytes 2574941 | solution.py:172
  (74 shorter events, 14.8 us)
Async XLA Ops:
  7.2 0.8 copy-start
  7.2 64.6 %all-gather.5.cloned.1.call-start = ((), (), s32[]{:S(2)}) async-start(), calls=%async_computation.2 | async-start | bytes 1179648 | tf_op jit(solution)/shard_map/all_gather | solution.py:119
  7.9 133.9 %all-gather.9.cloned.1.call-start = ((), (), s32[]{:S(2)}) async-start(), calls=%async_computation.4 | async-start | bytes 1064960 | tf_op jit(solution)/shard_map/all_gather | solution.py:134
  8.7 215.3 %all-gather.11.cloned.1.call-start = ((), (), s32[]{:S(2)}) async-start(), calls=%async_computation.5 | async-start | bytes 1064960 | tf_op jit(solution)/shard_map/all_gather | solution.py:139
  10.1 300.6 %all-gather.7.cloned.1.call-start = ((), (), s32[]{:S(2)}) async-start(), calls=%async_computation.3 | async-start | bytes 4259840 | tf_op jit(solution)/shard_map/all_gather | solution.py:129
  29.2 28.5 %all-to-all-start = ((s32[64,1,2]{2,1,0:T(1,128)}), s32[64,1,2]{2,1,0:T(1,128)S(1)}, u32[]{:S(2)}, u32[]{:S(2)}) async-start(s32[64,1,2]{2,1,0:T(1,128)} %bitcast.4), calls=%async_computation | async-start | bytes 65536 | tf_op jit(solution)/shard_map/all_to_all | solution.py:105
  55.8 14.4 %copy-start.2 = (s32[128]{0:T(128)S(1)}, s32[128]{0:T(128)}, u32[]{:S(2)}) copy-start(s32[128]{0:T(128)} %param.19) | copy-start | bytes 1540
  57.3 16.0 %copy-start.1 = (f32[4096]{0:T(1024)S(1)}, f32[4096]{0:T(1024)}, u32[]{:S(2)}) copy-start(f32[4096]{0:T(1024)} %param.12) | copy-start | bytes 49156
  57.8 41.9 %all-to-all-start.1 = ((bf16[64,2,4096]{2,1,0:T(2,128)(2,1)}), bf16[64,2,4096]{2,1,0:T(2,128)(2,1)S(1)}, u32[]{:S(2)}, u32[]{:S(2)}) async-start(bf16[64,2,4096]{2,1,0:T(2,128)(2,1)} %reshape.342), calls=%async_computation.1 | async-start | bytes 2097152 | tf_op jit(solution)/shard_map/all_to_all | solution.py:104
  104.1 121.5 %collective-permute-start = (bf16[4,1,2,256,128]{4,3,2,0,1:T(8,128)(2,1)S(1)}, bf16[4,1,2,256,128]{4,3,2,0,1:T(8,128)(2,1)S(1)}, u32[]{:S(2)}, u32[]{:S(2)}) collective-permute-start(bf16[4,1,2,256,128]{4,3,2,0,1:T(8,128)(2,1)S(1)} %bitcast_select_fusion), channel_id=1, source_target_pairs={{0,1},{1,0},{2,3},{3,2},{4,5},{5,4},{6,7},{7,6},{8,9},{9,8},{10,11... | collective-permute-start | bytes 1572872 | tf_op jit(solution)/shard_map/ppermute | solution.py:13
Sparse Core Ops, SparseCore 0:
  10.1 31.9 all-gather.4
  45.7 96.0 all-gather.8
  144.9 79.0 all-gather.10
  226.9 83.6 all-gather.6
where the time goes:
time: 327 us; the launch traced here: 326 us
  waiting for transfers between devices  227 us (69%)
  local copies, waits for them, and re-layouts  32 us (10%)
  starting transfers between devices  31.2 us (10%)
  between operations  14.2 us (4%)
  other arithmetic  12.5 us (4%)
  matrix products  8.96 us (3%)
    all_gather x1, waiting for transfers between devices, on_device(): lax.all_gather(q_weight, 'group', axis=0, tiled=True)  84.7 us
    all_gather x1, waiting for transfers between devices, on_device(): lax.all_gather(value_cols, 'group', axis=0, tiled=True)  80.1 us
    all_gather x1, waiting for transfers between devices, on_device(): lax.all_gather(key_cols, 'group', axis=0, tiled=True)  35.6 us
    all_to_all x1, waiting for transfers between devices, on_device(): lax.all_to_all(outgoing, 'group', split_axis=0, concat_axis=0, tiled=True)  24.7 us
    all_to_all x1, starting transfers between devices, on_device(): lax.all_to_all(outgoing_slots, 'group', split_axis=0, concat_axis=0, tile...  16.6 us
    scatter x1, local copies, waits for them, and re-layouts, on_device(): jnp.zeros((flat_table.shape[0],), jnp.int32).at[flat_table].set(slot_ids)  15.5 us
    all_to_all x1, starting transfers between devices, on_device(): lax.all_to_all(outgoing, 'group', split_axis=0, concat_axis=0, tiled=True)  12.4 us
  transfers between devices with their start and end apart: 7, of which 5 were waited for; matrix products, arithmetic and copies ran while one was open for 14% of the time, Pallas kernels for 0%

commit v1 on v0

--- a/solution.py
+++ b/solution.py
@@ -126,7 +126,15 @@
     value_cols = lax.dynamic_slice_in_dim(v_weight, first_kv * head_dim, head_dim, 1)
     query_sum = jnp.dot(
         normed,
-        lax.all_gather(q_weight, "group", axis=0, tiled=True),
+        jnp.concatenate(
+            lax.all_to_all(
+                jnp.stack([q_weight] * lax.psum(1, "group"), axis=0),
+                split_axis=0,
+                axis_name="group",
+                concat_axis=0,
+            ),
+            axis=0,
+        ),
         preferred_element_type=jnp.float32,
     )
     key_sum = jnp.dot(

time: 327 us -> 365 us (1.12)
  waiting for transfers between devices: 227 us -> 263 us
  local copies, waits for them, and re-layouts: 32 us -> 38.4 us
  other arithmetic: 12.5 us -> 8.07 us
    all_gather x1, waiting for transfers between devices: 35.6 us -> 145 us  [on_device(): lax.all_gather(key_cols, 'group', axis=0, tiled=True)]
    all_gather x1 -> x0, waiting for transfers between devices: 84.7 us -> none  [on_device(): lax.all_gather(q_weight, 'group', axis=0, tiled=True)]
    all_to_all x1, starting transfers between devices: 12.4 us -> 4.65 us  [on_device(): lax.all_to_all(outgoing, 'group', split_axis=0, concat_axis=0, tiled=True)]
    all_to_all x1, waiting for transfers between devices: 0.43 us -> 8.14 us  [on_device(): lax.all_to_all(outgoing_slots, 'group', split_axis=0, concat_axis=0, tile...]
    all_to_all x0 -> x1, starting transfers between devices: none -> 6.75 us  [on_device(): lax.all_to_all(jnp.stack([q_weight] * lax.psum(1, 'group'), axis=0), spli...]
    dot_general x0 -> x1, local copies, waits for them, and re-layouts: none -> 6.46 us  [on_device(): jnp.dot(normed, jnp.concatenate(lax.all_to_all(jnp.stack([q_weight] * lax...]
    all_to_all x1, waiting for transfers between devices: 24.7 us -> 28.4 us  [on_device(): lax.all_to_all(outgoing, 'group', split_axis=0, concat_axis=0, tiled=True)]
  transfers between devices with their start and end apart: 7 -> 7, of which waited for: 5 -> 4; matrix products, arithmetic and copies ran while one was open for 14% -> 6% of each run, Pallas kernels for 0% -> 0%
where the time goes in v1:
time: 365 us; the launch traced here: 364 us
  waiting for transfers between devices  263 us (72%)
  local copies, waits for them, and re-layouts  38.4 us (11%)
  starting transfers between devices  30.2 us (8%)
  between operations  14.2 us (4%)
  matrix products  9.92 us (3%)
  other arithmetic  8.07 us (2%)
    all_gather x1, waiting for transfers between devices, on_device(): lax.all_gather(key_cols, 'group', axis=0, tiled=True)  145 us
    all_gather x1, waiting for transfers between devices, on_device(): lax.all_gather(value_cols, 'group', axis=0, tiled=True)  80.5 us
    all_to_all x1, waiting for transfers between devices, on_device(): lax.all_to_all(outgoing, 'group', split_axis=0, concat_axis=0, tiled=True)  28.4 us
    all_to_all x1, starting transfers between devices, on_device(): lax.all_to_all(outgoing_slots, 'group', split_axis=0, concat_axis=0, tile...  16.6 us
    scatter x1, local copies, waits for them, and re-layouts, on_device(): jnp.zeros((flat_table.shape[0],), jnp.int32).at[flat_table].set(slot_ids)  15.5 us
    all_to_all x1, waiting for transfers between devices, on_device(): lax.all_to_all(outgoing_slots, 'group', split_axis=0, concat_axis=0, tile...  8.14 us
  transfers between devices with their start and end apart: 7, of which 4 were waited for; matrix products, arithmetic and copies ran while one was open for 6% of the time, Pallas kernels for 0%

profile of v1, /device:TPU:2, one launch (start us, length us, event | category | flops | bytes accessed | tf_op | source)
XLA Modules:
  0.0 364.0 jit_solution(10445298972479548596)
XLA Ops:
  7.2 0.8 copy.28
  8.2 15.5 %scatter_custom_fusion = s32[4096]{0:T(1024)S(1)} fusion(s32[4096]{0:T(1024)S(1)} %bitcast.81, s32[4096]{0:T(1024)S(1)} %iota.46, s32[]{:T(128)} %copy.59), kind=kCustom, calls=%fused_computation.81 | custom fusion | bytes 16388 | tf_op jit(solution)/shard_map/scatter | solution.py:80
  24.3 0.8 scatter_custom_fusion.1
  25.8 16.6 %all-to-all-start.1 = ((s32[64,1,2]{2,1,0:T(1,128)}), s32[64,1,2]{2,1,0:T(1,128)S(1)}, u32[]{:S(2)}, u32[]{:S(2)}) async-start(s32[64,1,2]{2,1,0:T(1,128)} %bitcast.8), calls=%async_computation.1 | async-start | bytes 65536 | tf_op jit(solution)/shard_map/all_to_all | solution.py:105
  42.4 2.3 scatter_custom_fusion.2
  44.7 1.5 reshape.346
  46.2 8.1 %all-to-all-done.1 = s32[64,1,2]{2,1,0:T(1,128)S(1)} async-done(((s32[64,1,2]{2,1,0:T(1,128)}), s32[64,1,2]{2,1,0:T(1,128)S(1)}, u32[]{:S(2)}, u32[]{:S(2)}) %all-to-all-start.1) | async-done | bytes 544 | tf_op jit(solution)/shard_map/all_to_all | solution.py:105
  54.3 4.7 %all-to-all-start.2 = ((bf16[64,2,4096]{2,1,0:T(2,128)(2,1)}), bf16[64,2,4096]{2,1,0:T(2,128)(2,1)S(1)}, u32[]{:S(2)}, u32[]{:S(2)}) async-start(bf16[64,2,4096]{2,1,0:T(2,128)(2,1)} %reshape.346), calls=%async_computation.2 | async-start | bytes 2097152 | tf_op jit(solution)/shard_map/all_to_all | solution.py:104
  59.7 28.4 %all-to-all-done.2 = bf16[64,2,4096]{2,1,0:T(2,128)(2,1)S(1)} async-done(((bf16[64,2,4096]{2,1,0:T(2,128)(2,1)}), bf16[64,2,4096]{2,1,0:T(2,128)(2,1)S(1)}, u32[]{:S(2)}, u32[]{:S(2)}) %all-to-all-start.2) | async-done | bytes 1048608 | tf_op jit(solution)/shard_map/all_to_all | solution.py:104
  88.2 2.5 stack.2
  90.6 6.7 %all-to-all-start = ((bf16[64,64,512]{2,1,0:T(8,128)(2,1)}), bf16[64,64,512]{2,1,0:T(8,128)(2,1)}, u32[]{:S(2)}, u32[]{:S(2)}) async-start(bf16[64,64,512]{2,1,0:T(8,128)(2,1)} %stack.2), calls=%async_computation | async-start | bytes 8388608 | tf_op jit(solution)/shard_map/all_to_all | solution.py:130
  98.2 1.3 constant_dynamic-slice_fusion
  100.5 2.6 compare_select_fusion.2
  105.4 1.5 fusion.7
  107.3 2.1 scatter_custom_fusion.3
  109.9 2.1 collective-permute-start
  112.0 145.2 %all-gather.6.cloned.1.call-done = bf16[4096,128]{1,0:T(8,128)(2,1)} async-done(((bf16[64,128]{1,0:T(8,128)(2,1)}), bf16[4096,128]{1,0:T(8,128)(2,1)}) %all-gather.6.cloned.1.call-update) | async-done | bytes 1048592 | tf_op jit(solution)/shard_map/all_gather | solution.py:142
  257.2 1.9 convolution_bitcast_fusion
  259.4 80.5 %all-gather.8.cloned.1.call-done = bf16[4096,128]{1,0:T(8,128)(2,1)} async-done(((bf16[64,128]{1,0:T(8,128)(2,1)}), bf16[4096,128]{1,0:T(8,128)(2,1)}) %all-gather.8.cloned.1.call-update) | async-done | bytes 1048592 | tf_op jit(solution)/shard_map/all_gather | solution.py:147
  340.0 1.8 convolution_convert_fusion.1
  342.1 6.5 %copy.27 = bf16[512,4096]{1,0:T(8,128)(2,1)} copy(bf16[512,4096]{0,1:T(8,128)(2,1)} %bitcast.4) | data formatting | bytes 8388608 | tf_op jit(solution)/shard_map/dot_general | solution.py:127
  348.5 3.5 fusion.10
  352.1 3.9 %while.10 = (s32[]{:T(128)}, bf16[4,128,128]{2,1,0:T(8,128)(2,1)S(1)}, bf16[4,128,128]{1,2,0:T(8,128)(2,1)S(1)}, bf16[1152,128]{1,0:T(8,128)(2,1)S(1)}, pred[128...) while((s32[]{:T(128)}, bf16[4,128,128]{2,1,0:T(8,128)(2,1)S(1)}, ...), condition=%wide.region_13.14_spmd, body=%wide.region_10.13_spmd.sunk | while | flops 76693248 | bytes 2574941 | solution.py:180
  356.7 0.8 copy.60
  (78 shorter events, 12.0 us)
Async XLA Ops:
  7.2 90.3 %copy-start = (bf16[64,512]{1,0:T(8,128)(2,1)S(1)}, bf16[64,512]{1,0:T(8,128)(2,1)}, u32[]{:S(2)}) copy-start(bf16[64,512]{1,0:T(8,128)(2,1)} %param.14) | copy-start | bytes 196612
  25.8 28.5 %all-to-all-start.1 = ((s32[64,1,2]{2,1,0:T(1,128)}), s32[64,1,2]{2,1,0:T(1,128)S(1)}, u32[]{:S(2)}, u32[]{:S(2)}) async-start(s32[64,1,2]{2,1,0:T(1,128)} %bitcast.8), calls=%async_computation.1 | async-start | bytes 65536 | tf_op jit(solution)/shard_map/all_to_all | solution.py:105
  44.7 43.5 %copy-start.2 = (bf16[64,512]{1,0:T(8,128)(2,1)S(1)}, bf16[64,512]{1,0:T(8,128)(2,1)}, u32[]{:S(2)}) copy-start(bf16[64,512]{1,0:T(8,128)(2,1)} %param.13) | copy-start | bytes 196612
  54.3 33.8 %all-to-all-start.2 = ((bf16[64,2,4096]{2,1,0:T(2,128)(2,1)}), bf16[64,2,4096]{2,1,0:T(2,128)(2,1)S(1)}, u32[]{:S(2)}, u32[]{:S(2)}) async-start(bf16[64,2,4096]{2,1,0:T(2,128)(2,1)} %reshape.346), calls=%async_computation.2 | async-start | bytes 2097152 | tf_op jit(solution)/shard_map/all_to_all | solution.py:104
  59.0 46.4 %all-gather.4.cloned.1.call-start = ((), (), s32[]{:S(2)}) async-start(), calls=%async_computation.3 | async-start | bytes 1179648 | tf_op jit(solution)/shard_map/all_gather | solution.py:119
  90.6 8.9 %copy-start.3 = (s32[128]{0:T(128)S(1)}, s32[128]{0:T(128)}, u32[]{:S(2)}) copy-start(s32[128]{0:T(128)} %param.19) | copy-start | bytes 1540
  90.6 9.2 %copy-start.4 = (s32[4]{0:T(128)S(1)}, s32[4]{0:T(128)}, u32[]{:S(2)}) copy-start(s32[4]{0:T(128)} %param.18) | copy-start | bytes 52
  90.6 251.4 %all-to-all-start = ((bf16[64,64,512]{2,1,0:T(8,128)(2,1)}), bf16[64,64,512]{2,1,0:T(8,128)(2,1)}, u32[]{:S(2)}, u32[]{:S(2)}) async-start(bf16[64,64,512]{2,1,0:T(8,128)(2,1)} %stack.2), calls=%async_computation | async-start | bytes 8388608 | tf_op jit(solution)/shard_map/all_to_all | solution.py:130
  97.4 159.8 %all-gather.6.cloned.1.call-start = ((), (), s32[]{:S(2)}) async-start(), calls=%async_computation.4 | async-start | bytes 1064960 | tf_op jit(solution)/shard_map/all_gather | solution.py:142
  98.1 241.8 %all-gather.8.cloned.1.call-start = ((), (), s32[]{:S(2)}) async-start(), calls=%async_computation.5 | async-start | bytes 1064960 | tf_op jit(solution)/shard_map/all_gather | solution.py:147
  109.5 147.8 %copy-start.1 = (bf16[128,4096]{1,0:T(8,128)(2,1)S(1)}, bf16[128,4096]{1,0:T(8,128)(2,1)}, u32[]{:S(2)}) copy-start(bf16[128,4096]{1,0:T(8,128)(2,1)} %all-gather.4.cloned.1.call-done) | copy-start | bytes 3145732
  109.5 147.8 %copy-start.5 = (f32[4096]{0:T(1024)S(1)}, f32[4096]{0:T(1024)}, u32[]{:S(2)}) copy-start(f32[4096]{0:T(1024)} %param.12) | copy-start | bytes 49156
  109.9 231.9 %collective-permute-start = (bf16[4,1,2,256,128]{4,3,2,0,1:T(8,128)(2,1)S(1)}, bf16[4,1,2,256,128]{4,3,2,0,1:T(8,128)(2,1)S(1)}, u32[]{:S(2)}, u32[]{:S(2)}) collective-permute-start(bf16[4,1,2,256,128]{4,3,2,0,1:T(8,128)(2,1)S(1)} %bitcast_select_fusion), channel_id=1, source_target_pairs={{0,1},{1,0},{2,3},{3,2},{4,5},{5,4},{6,7},{7,6},{8,9},{9,8},{10,11... | collective-permute-start | bytes 1572872 | tf_op jit(solution)/shard_map/ppermute | solution.py:13
Sparse Core Ops, SparseCore 0:
  61.9 28.1 all-gather.3
  101.8 155.3 all-gather.5
  260.9 79.0 all-gather.7
